TPU v7x, 256 devices: a whole 4x4x8 slice. The times are simulated.
256 devices in a mesh: dp: 4 (over z_lo, core), cp: 16 (over y, z_hi), tp: 4 (over x).
Axes of the slice: x: 4, y: 4, z: 8 (z_hi: 4, z_lo: 2; z = z_hi * 2 + z_lo), core: 2. Of those that a mesh axis runs over, the one named last changes fastest.
Arguments:
- hidden: bfloat16 [4, 2048, 8192], P('dp', 'cp'), may hold values from -6 to 6
- query: bfloat16 [4, 2048, 8192], P('dp', 'cp', 'tp'), may hold values from -360 to 360
- grad_out: bfloat16 [4, 2048, 8192], P('dp', 'cp', 'tp'), may hold values from -6 to 6
- k_weight: bfloat16 [8192, 1024], P('dp', 'tp'), may hold values from -0.0625 to 0.0625
- v_weight: bfloat16 [8192, 1024], P('dp', 'tp'), may hold values from -0.0625 to 0.0625
- doc_starts: int32 [4, 4], P('dp'), may hold values from 0 to 2047, as said below
Outputs:
- attn_out: bfloat16 [4, 2048, 8192], P('dp', 'cp', 'tp')
- query_grad: bfloat16 [4, 2048, 8192], P('dp', 'cp', 'tp')
- k_weight_grad: float32 [8192, 1024], P(('dp', 'cp'), 'tp')
- v_weight_grad: float32 [8192, 1024], P(('dp', 'cp'), 'tp')
Inputs may be any that keep to these rules, and one draw needn't show every extreme that they name: `doc_starts`: in each sequence the starts strictly increase and the first is 0.
All inputs are finite; a program needn't handle non-finite values.
Results may differ from a plain program's by a relative error of at most 0.04.
The roundings to bfloat16 on the way count: a program that leaves them out, or rounds other values in their place, can miss the bound.
Values may be sent and summed in bfloat16 or wider, within the bound.
No kernel may reach another device: no remote copies, remote signals or barrier semaphores. Data moves between devices by JAX's collectives and lax.ppermute only.
A program may use at most 128 MiB of HBM per device.

v0:
```python
import jax
import jax.numpy as jnp
from jax import lax
from jax.sharding import PartitionSpec as P

DH = 128
NEG_BIG = -1e30


def place(rows, tok_rows, seq_rows):
    stretch = rows // tok_rows
    within = rows % tok_rows
    half_rows = tok_rows // 2
    return jnp.where(
        within < half_rows,
        stretch * half_rows + within,
        seq_rows - (stretch + 1) * half_rows + within - half_rows,
    )


def doc_index(positions, starts):
    return jnp.sum((starts[None, :] <= positions[:, None]).astype(jnp.int32), axis=1) - 1


def on_device(hidden, query, grad_out, k_weight, v_weight, doc_starts):
    inputs = hidden[0]
    tok_rows, width = inputs.shape
    cp_count = lax.axis_size("cp")
    dp_count = lax.axis_size("dp")
    seq_rows = tok_rows * cp_count
    score_scale = DH ** (-0.5)
    kv_width = k_weight.shape[1]
    kv_heads = kv_width // DH
    per_group = query.shape[2] // DH // kv_heads
    starts = doc_starts[0]
    blk = width // (dp_count * cp_count)
    cols = inputs.reshape(tok_rows, dp_count, cp_count, blk).transpose(2, 0, 1, 3)
    cols = lax.all_to_all(cols, "cp", 0, 0, tiled=True)
    both_w = jnp.concatenate([k_weight, v_weight], axis=1)
    both_w = lax.all_gather(both_w, "dp", axis=0, tiled=True)
    kv = jnp.dot(inputs, both_w, preferred_element_type=jnp.float32).astype(jnp.bfloat16)
    kv_all = lax.all_gather(kv, "cp", axis=0, tiled=True)
    key_heads = kv_all[:, :kv_width].reshape(seq_rows, kv_heads, DH)
    value_heads = kv_all[:, kv_width:].reshape(seq_rows, kv_heads, DH)
    own_rows = lax.axis_index("cp") * tok_rows + jnp.arange(tok_rows, dtype=jnp.int32)
    own_place = place(own_rows, tok_rows, seq_rows)
    own_doc = doc_index(own_place, starts)
    key_place = place(jnp.arange(seq_rows, dtype=jnp.int32), tok_rows, seq_rows)
    key_doc = doc_index(key_place, starts)
    allowed = (key_place[None, :] <= own_place[:, None]) & (key_doc[None, :] == own_doc[:, None])
    queries = query[0].reshape(tok_rows, kv_heads, per_group, DH)
    upstream = grad_out[0].reshape(tok_rows, kv_heads, per_group, DH)
    scores = (
        jnp.einsum("qgid,kgd->giqk", queries, key_heads, preferred_element_type=jnp.float32)
        * score_scale
    )
    scores = jnp.where(allowed, scores, NEG_BIG)
    top_score = jnp.max(scores, axis=-1)
    expos = jnp.where(allowed, jnp.exp(scores - top_score[..., None]), 0.0)
    log_total = top_score + jnp.log(jnp.sum(expos, axis=-1))
    weights = jnp.where(allowed, jnp.exp(scores - log_total[..., None]), 0.0)
    weights_bf = weights.astype(jnp.bfloat16)
    out_rows = jnp.einsum(
        "giqk,kgd->qgid", weights_bf, value_heads, preferred_element_type=jnp.float32
    ).astype(jnp.bfloat16)
    delta = jnp.transpose(
        jnp.sum(upstream.astype(jnp.float32) * out_rows.astype(jnp.float32), axis=-1), (1, 2, 0)
    )
    prob_grads = jnp.einsum(
        "qgid,kgd->giqk", upstream, value_heads, preferred_element_type=jnp.float32
    )
    score_grads = (weights * (prob_grads - delta[..., None])).astype(jnp.bfloat16)
    query_acc = (
        jnp.einsum("giqk,kgd->qgid", score_grads, key_heads, preferred_element_type=jnp.float32)
        * score_scale
    )
    key_term = (
        jnp.einsum("giqk,qgid->kgd", score_grads, queries, preferred_element_type=jnp.float32)
        * score_scale
    )
    value_term = jnp.einsum(
        "giqk,qgid->kgd", weights_bf, upstream, preferred_element_type=jnp.float32
    )
    both_terms = jnp.concatenate(
        [key_term.reshape(seq_rows, kv_width), value_term.reshape(seq_rows, kv_width)], axis=1
    ).astype(jnp.bfloat16)
    both_grads = lax.psum(both_terms, "cp")
    grads = both_grads.reshape(cp_count, tok_rows, 2 * kv_width)
    partial = jnp.einsum("ctjb,ctn->jbn", cols, grads, preferred_element_type=jnp.float32)
    result = lax.psum_scatter(partial, "dp", scatter_dimension=0, tiled=True)[0]
    attn_rows = out_rows.reshape(1, tok_rows, kv_heads * per_group * DH)
    query_rows = query_acc.astype(jnp.bfloat16).reshape(1, tok_rows, kv_heads * per_group * DH)
    return (attn_rows, query_rows, result[:, :kv_width], result[:, kv_width:])


def solution(mesh):
    placed = (
        P("dp", "cp", None),
        P("dp", "cp", "tp"),
        P("dp", "cp", "tp"),
        P("dp", "tp"),
        P("dp", "tp"),
        P("dp", None),
    )
    return jax.shard_map(
        on_device,
        mesh=mesh,
        in_specs=placed,
        out_specs=(
            P("dp", "cp", "tp"),
            P("dp", "cp", "tp"),
            P(("dp", "cp"), "tp"),
            P(("dp", "cp"), "tp"),
        ),
        check_vma=False,
    )
```

profile of v0, /device:TPU:1, one launch (start us, length us, event | category | flops | bytes accessed | tf_op | source)
XLA Modules:
  0.0 460.0 jit_solution(11077758612200397458)
XLA Ops:
  7.2 3.1 pad_maximum_fusion
  10.3 88.3 %all-gather.3.cloned.1.call-done = bf16[8192,512]{1,0:T(8,128)(2,1)} async-done(((bf16[2048,512]{1,0:T(8,128)(2,1)}), bf16[8192,512]{1,0:T(8,128)(2,1)}) %all-gather.3.cloned.1.call-update) | async-done | bytes 8388624 | tf_op jit(solution)/shard_map/all_gather | solution.py:40
  98.7 7.0 %fusion.18 = bf16[128,512]{0,1:T(8,128)(2,1)} fusion(bf16[8192,512]{1,0:T(8,128)(2,1)} %all-gather.3.cloned.1.call-done, bf16[1,128,8192]{2,1,0:T(8,128)(2,1)} %param.6), kind=kOutput, calls=%fused_computation.24 | convolution fusion | flops 1073807360 | bytes 10616832 | tf_op jit(solution)/shard_map/dot_general | solution.py:41
  105.7 3.3 copy.76
  109.0 2.6 copy.77
  111.6 8.4 %all-to-all-start = ((bf16[16,128,4,128]{3,1,2,0:T(8,128)(2,1)}), bf16[16,128,4,128]{3,1,2,0:T(8,128)(2,1)}, u32[]{:S(2)}, u32[]{:S(2)}) async-start(bf16[16,128,4,128]{3,1,2,0:T(8,128)(2,1)} %copy.77), calls=%async_computation | async-start | bytes 4194304 | tf_op jit(solution)/shard_map/all_to_all | solution.py:38
  120.3 0.3 copy.99
  120.6 1.0 copy.66
  121.9 1.3 compare_and_fusion
  123.2 66.3 %all-gather.5.cloned.1.call-done = bf16[2048,512]{0,1:T(8,128)(2,1)} async-done(((bf16[128,512]{0,1:T(8,128)(2,1)}), bf16[2048,512]{0,1:T(8,128)(2,1)}) %all-gather.5.cloned.1.call-update) | async-done | bytes 2097168 | tf_op jit(solution)/shard_map/all_gather | solution.py:42
  189.5 2.7 fusion.39
  192.2 2.6 fusion.3
  194.8 4.0 select_reduce_fusion
  198.8 1.7 copy-done
  200.6 8.2 %fusion.6 = bf16[2,2048,128]{1,2,0:T(8,128)(2,1)S(1)} fusion(bf16[128,2,8,128]{0,3,2,1:T(8,128)(2,1)S(1)} %bitcast.117, f32[2,2048,128,8]{2,1,3,0:T(8,128)} %copy-done, f32[2,8,128]{2,1,0:T(8,128)S(1)} %log_add_fusion, pred[128,2048]{0,1:T(8,128)(4,1)S(1)} %compare_and_fusion), kind=kOutput, calls=%fused_computation.12 | convolution fusion | flops 1095237632 | bytes 18620416 | tf_op jit(solution)/shard_map/giqk,qgid->kgd/dot_general | solution.py:81
  208.8 1.3 copy.74
  210.1 11.1 %multiply_reduce_fusion = (f32[128,2,8]{0,2,1:T(8,128)S(1)}, bf16[2,128,8,128]{3,1,2,0:T(8,128)(2,1)}) fusion(bf16[128,2,8,128]{0,3,2,1:T(8,128)(2,1)S(1)} %bitcast.118, bf16[2048,2,128,1]{0,2,3,1:T(8,128)(2,1)} %bitcast.114, f32[2,2048,128,8]{2,1,3,0:T(8,128)} %copy-done, f32[2,8,128]{2,1,0:T(8,128)S(1)} %log_add_fusion, ...), kind=kOutput, calls=%fused_computation.25 | convolution fusion | flops 1096022016 | bytes 19152896 | tf_op jit(solution)/shard_map/giqk,kgd->qgid/dot_general | solution.py:63
  221.3 9.3 %fusion.1 = bf16[2,8,128,2048]{2,3,1,0:T(8,128)(2,1)S(1)} fusion(f32[2,2048,128,8]{2,1,3,0:T(8,128)} %copy-done, f32[2,8,128]{2,1,0:T(8,128)S(1)} %bitcast.123, f32[2,8,128]{2,1,0:T(8,128)S(1)} %log_add_fusion, pred[128,2048]{0,1:T(8,128)(4,1)S(1)} %compare_and_fusion, bf16[2048,2,128,1]{0,2,3,1:T(8,128)(2,1)S(1)} %bitcast.115, ...), kind=kOutput, calls=%fused_computation.2 | convolution fusion | flops 1103101952 | bytes 27017216 | tf_op jit(solution)/shard_map/qgid,kgd->giqk/dot_general | solution.py:69
  230.5 3.2 copy-done.1
  233.7 2.8 fusion.5
  236.6 1.3 copy.73
  237.9 1.7 pad_maximum_fusion.1
  239.6 2.4 copy.75
  242.1 174.2 %all-reduce.2.cloned.1.call-done = bf16[16,128,512]{1,2,0:T(8,128)(2,1)} async-done(((bf16[16,128,512]{1,2,0:T(8,128)(2,1)}), bf16[16,128,512]{1,2,0:T(8,128)(2,1)}) %all-reduce.2.cloned.1.call-update) | async-done | bytes 2097168 | tf_op jit(solution)/shard_map/psum | solution.py:87
  416.3 4.4 fusion.11
  420.8 4.7 %fusion.14 = bf16[2,128,8,128]{3,1,2,0:T(8,128)(2,1)S(1)} fusion(bf16[2048,2,128,1]{0,2,3,1:T(8,128)(2,1)S(1)} %bitcast.106, bf16[2,8,128,2048]{2,3,1,0:T(8,128)(2,1)} %copy-done.1), kind=kOutput, calls=%fused_computation.21 | convolution fusion | flops 1074266112 | bytes 9961472 | tf_op jit(solution)/shard_map/giqk,kgd->qgid/dot_general | solution.py:74
  425.5 1.0 copy.80
  426.5 1.0 copy.79
  427.5 23.4 %reduce-scatter.2.cloned.1.call-done = f32[1,128,512]{1,2,0:T(8,128)} async-done(((f32[4,128,512]{1,2,0:T(8,128)}), f32[1,128,512]{1,2,0:T(8,128)}) %reduce-scatter.2.cloned.1.call-update) | async-done | bytes 262160 | tf_op jit(solution)/shard_map/reduce_scatter | solution.py:90
  451.0 1.0 fusion.40
  452.0 0.8 copy.81
  452.7 0.8 copy.82
  (30 shorter events, 0.7 us)
Async XLA Ops:
  7.2 91.5 %all-gather.3.cloned.1.call-start = ((), (), s32[]{:S(2)}) async-start(), calls=%async_computation.2 | async-start | bytes 10485760 | tf_op jit(solution)/shard_map/all_gather | solution.py:40
  10.3 179.2 %all-gather.5.cloned.1.call-start = ((), (), s32[]{:S(2)}) async-start(), calls=%async_computation.3 | async-start | bytes 2228224 | tf_op jit(solution)/shard_map/all_gather | solution.py:42
  105.7 14.6 %copy-start.3 = (bf16[1,128,2048]{2,1,0:T(8,128)(2,1)S(1)}, bf16[1,128,2048]{2,1,0:T(8,128)(2,1)}, u32[]{:S(2)}) copy-start(bf16[1,128,2048]{2,1,0:T(8,128)(2,1)} %param.7) | copy-start | bytes 1572868
  105.7 14.9 %copy-start.4 = (bf16[1,128,2048]{2,1,0:T(8,128)(2,1)S(1)}, bf16[1,128,2048]{2,1,0:T(8,128)(2,1)}, u32[]{:S(2)}) copy-start(bf16[1,128,2048]{2,1,0:T(8,128)(2,1)} %param.8) | copy-start | bytes 1572868
  105.7 16.0 %copy-start.7 = (s32[1,4]{1,0:T(1,128)S(1)}, s32[1,4]{1,0:T(1,128)}, u32[]{:S(2)}) copy-start(s32[1,4]{1,0:T(1,128)} %param.11) | copy-start | bytes 52
  111.6 130.4 %all-to-all-start = ((bf16[16,128,4,128]{3,1,2,0:T(8,128)(2,1)}), bf16[16,128,4,128]{3,1,2,0:T(8,128)(2,1)}, u32[]{:S(2)}, u32[]{:S(2)}) async-start(bf16[16,128,4,128]{3,1,2,0:T(8,128)(2,1)} %copy.77), calls=%async_computation | async-start | bytes 4194304 | tf_op jit(solution)/shard_map/all_to_all | solution.py:38
  120.1 296.2 %all-reduce.2.cloned.1.call-start = ((), (), s32[]{:S(2)}) async-start(), calls=%async_computation.4 | async-start | bytes 4194304 | tf_op jit(solution)/shard_map/psum | solution.py:87
  194.8 5.7 %copy-start = (f32[2,2048,128,8]{2,1,3,0:T(8,128)}, f32[2,2048,128,8]{2,1,3,0:T(8,128)S(1)}, u32[]{:S(2)}) copy-start(f32[2,2048,128,8]{2,1,3,0:T(8,128)S(1)} %get-tuple-element.25) | copy-start | bytes 50331652
  194.8 5.7 %copy-start.6 = (bf16[1,128,2048]{1,2,0:T(8,128)(2,1)S(1)}, bf16[1,128,2048]{1,2,0:T(8,128)(2,1)}, u32[]{:S(2)}) copy-start(bf16[1,128,2048]{1,2,0:T(8,128)(2,1)} %copy.66) | copy-start | bytes 1572868
  210.1 11.1 %copy-start.2 = (bf16[2048,256]{0,1:T(8,128)(2,1)S(1)}, bf16[2048,256]{0,1:T(8,128)(2,1)}, u32[]{:S(2)}) copy-start(bf16[2048,256]{0,1:T(8,128)(2,1)} %get-tuple-element.21) | copy-start | bytes 3145732
  230.5 3.2 copy-start.1
  242.0 208.9 %reduce-scatter.2.cloned.1.call-start = ((), (), s32[]{:S(2)}) async-start(), calls=%async_computation.5 | async-start | bytes 1310720 | tf_op jit(solution)/shard_map/reduce_scatter | solution.py:90
  420.8 5.7 %copy-start.5 = (bf16[2,128,8,128]{3,1,2,0:T(8,128)(2,1)S(1)}, bf16[2,128,8,128]{3,1,2,0:T(8,128)(2,1)}, u32[]{:S(2)}) copy-start(bf16[2,128,8,128]{3,1,2,0:T(8,128)(2,1)} %get-tuple-element.27) | copy-start | bytes 1572868
Sparse Core Ops, SparseCore 0:
  10.4 88.2 all-gather.2
  105.8 83.6 all-gather.4
  242.2 174.1 all-reduce.1
  420.9 30.0 reduce-scatter.1
where the time goes:
time: 460 us
  waiting for transfers between devices  352 us (77%)
  matrix products  50.2 us (11%)
  local copies, waits for them, and re-layouts  24.5 us (5%)
  between operations  14 us (3%)
  other arithmetic  10.3 us (2%)
  starting transfers between devices  8.78 us (2%)
    psum x1, waiting for transfers between devices, on_device(): both_grads = lax.psum(both_terms, 'cp')  174 us
    all_gather x1, waiting for transfers between devices, on_device(): both_w = lax.all_gather(both_w, 'dp', axis=0, tiled=True)  88.3 us
    all_gather x1, waiting for transfers between devices, on_device(): kv_all = lax.all_gather(kv, 'cp', axis=0, tiled=True)  66.3 us
    reduce_scatter x1, waiting for transfers between devices, on_device(): result = lax.psum_scatter(partial, 'dp', scatter_dimension=0, tiled=True)[0]  23.4 us
    unnamed x22, local copies, waits for them, and re-layouts  12.8 us
    dot_general x1, matrix products, on_device(): jnp.einsum('giqk,kgd->qgid', weights_bf, value_heads, preferred_element_t...  11.1 us
    dot_general x1, matrix products, on_device(): jnp.einsum('qgid,kgd->giqk', upstream, value_heads, preferred_element_typ...  9.25 us
  transfers between devices with their start and end apart: 5, of which 4 were waited for; matrix products, arithmetic and copies ran while one was open for 14% of the time, Pallas kernels for 0%

commit v1 on v0

--- a/solution.py
+++ b/solution.py
@@ -39,7 +39,9 @@
     both_w = jnp.concatenate([k_weight, v_weight], axis=1)
     both_w = lax.all_gather(both_w, "dp", axis=0, tiled=True)
     kv = jnp.dot(inputs, both_w, preferred_element_type=jnp.float32).astype(jnp.bfloat16)
-    kv_all = lax.all_gather(kv, "cp", axis=0, tiled=True)
+    kv_all = jnp.concatenate(
+        lax.all_to_all(jnp.stack([kv] * lax.axis_size("cp")), "cp", 0, 0), axis=0
+    )
     key_heads = kv_all[:, :kv_width].reshape(seq_rows, kv_heads, DH)
     value_heads = kv_all[:, kv_width:].reshape(seq_rows, kv_heads, DH)
     own_rows = lax.axis_index("cp") * tok_rows + jnp.arange(tok_rows, dtype=jnp.int32)

time: 460 us -> 441 us (0.959)
  waiting for transfers between devices: 352 us -> 324 us
  starting transfers between devices: 8.78 us -> 13.4 us
    all_gather x1 -> x0, waiting for transfers between devices: 66.3 us -> none  [on_device(): kv_all = lax.all_gather(kv, 'cp', axis=0, tiled=True)]
    all_to_all x0 -> x1, waiting for transfers between devices: none -> 38.9 us  [on_device(): lax.all_to_all(jnp.stack([kv] * lax.axis_size('cp')), 'cp', 0, 0)]
    all_to_all x0 -> x1, starting transfers between devices: none -> 8.39 us  [on_device(): lax.all_to_all(jnp.stack([kv] * lax.axis_size('cp')), 'cp', 0, 0)]
  transfers between devices with their start and end apart: 5 -> 5, of which waited for: 4 -> 4; matrix products, arithmetic and copies ran while one was open for 14% -> 15% of each run, Pallas kernels for 0% -> 0%
where the time goes in v1:
time: 441 us; the launch traced here: 440 us
  waiting for transfers between devices  324 us (73%)
  matrix products  52.1 us (12%)
  local copies, waits for them, and re-layouts  26.7 us (6%)
  between operations  14 us (3%)
  starting transfers between devices  13.4 us (3%)
  other arithmetic  10.4 us (2%)
    psum x1, waiting for transfers between devices, on_device(): both_grads = lax.psum(both_terms, 'cp')  173 us
    all_gather x1, waiting for transfers between devices, on_device(): both_w = lax.all_gather(both_w, 'dp', axis=0, tiled=True)  88.4 us
    all_to_all x1, waiting for transfers between devices, on_device(): lax.all_to_all(jnp.stack([kv] * lax.axis_size('cp')), 'cp', 0, 0)  38.9 us
    reduce_scatter x1, waiting for transfers between devices, on_device(): result = lax.psum_scatter(partial, 'dp', scatter_dimension=0, tiled=True)[0]  23.4 us
    unnamed x22, local copies, waits for them, and re-layouts  13.4 us
    dot_general x1, matrix products, on_device(): jnp.einsum('giqk,kgd->qgid', weights_bf, value_heads, preferred_element_t...  10.8 us
    dot_general x1, matrix products, on_device(): jnp.einsum('giqk,qgid->kgd', weights_bf, upstream, preferred_element_type...  10.1 us
    dot_general x1, matrix products, on_device(): jnp.einsum('qgid,kgd->giqk', upstream, value_heads, preferred_element_typ...  9.28 us
  transfers between devices with their start and end apart: 5, of which 4 were waited for; matrix products, arithmetic and copies ran while one was open for 15% of the time, Pallas kernels for 0%

profile of v1, /device:TPU:1, one launch (start us, length us, event | category | flops | bytes accessed | tf_op | source)
XLA Modules:
  0.0 440.4 jit_solution(13827910349693783425)
XLA Ops:
  7.2 3.0 pad_maximum_fusion
  10.3 88.4 %all-gather.2.cloned.1.call-done = bf16[8192,512]{1,0:T(8,128)(2,1)} async-done(((bf16[2048,512]{1,0:T(8,128)(2,1)}), bf16[8192,512]{1,0:T(8,128)(2,1)}) %all-gather.2.cloned.1.call-update) | async-done | bytes 8388624 | tf_op jit(solution)/shard_map/all_gather | solution.py:40
  98.6 6.3 %fusion.18 = bf16[128,512]{0,1:T(8,128)(2,1)S(1)} fusion(bf16[8192,512]{1,0:T(8,128)(2,1)} %all-gather.2.cloned.1.call-done, bf16[1,128,8192]{2,1,0:T(8,128)(2,1)} %param.6), kind=kOutput, calls=%fused_computation.25 | convolution fusion | flops 1073807360 | bytes 10616832 | tf_op jit(solution)/shard_map/dot_general | solution.py:41
  105.0 1.7 stack.2
  106.8 8.4 %all-to-all-start = ((bf16[16,128,512]{1,2,0:T(8,128)(2,1)}), bf16[16,128,512]{1,2,0:T(8,128)(2,1)S(1)}, u32[]{:S(2)}, u32[]{:S(2)}) async-start(bf16[16,128,512]{1,2,0:T(8,128)(2,1)} %stack.2), calls=%async_computation | async-start | bytes 4194304 | tf_op jit(solution)/shard_map/all_to_all | solution.py:43
  115.2 4.1 copy.78
  119.2 1.0 copy.101
  120.2 1.0 copy.68
  121.2 3.9 copy.79
  125.4 1.3 compare_and_fusion
  126.8 38.9 %all-to-all-done = bf16[16,128,512]{1,2,0:T(8,128)(2,1)S(1)} async-done(((bf16[16,128,512]{1,2,0:T(8,128)(2,1)}), bf16[16,128,512]{1,2,0:T(8,128)(2,1)S(1)}, u32[]{:S(2)}, u32[]{:S(2)}) %all-to-all-start) | async-done | bytes 2097184 | tf_op jit(solution)/shard_map/all_to_all | solution.py:43
  165.6 4.9 %all-to-all-start.1 = ((bf16[16,128,4,128]{3,1,2,0:T(8,128)(2,1)}), bf16[16,128,4,128]{3,1,2,0:T(8,128)(2,1)}, u32[]{:S(2)}, u32[]{:S(2)}) async-start(bf16[16,128,4,128]{3,1,2,0:T(8,128)(2,1)} %copy.79), calls=%async_computation.1 | async-start | bytes 4194304 | tf_op jit(solution)/shard_map/all_to_all | solution.py:38
  171.0 3.6 fusion.3
  174.6 4.2 select_reduce_fusion
  178.8 1.5 copy-done
  180.4 10.1 %fusion.6 = bf16[2,2048,128]{1,2,0:T(8,128)(2,1)S(1)} fusion(bf16[128,2,8,128]{0,3,2,1:T(8,128)(2,1)} %bitcast.121, f32[2,2048,128,8]{2,1,3,0:T(8,128)} %copy-done, f32[2,8,128]{2,1,0:T(8,128)S(1)} %log_add_fusion, pred[128,2048]{0,1:T(8,128)(4,1)S(1)} %compare_and_fusion), kind=kOutput, calls=%fused_computation.12 | convolution fusion | flops 1095237632 | bytes 18620416 | tf_op jit(solution)/shard_map/giqk,qgid->kgd/dot_general | solution.py:83
  190.4 1.3 copy.76
  191.8 10.8 %multiply_reduce_fusion = (f32[128,2,8]{0,2,1:T(8,128)S(1)}, bf16[2,128,8,128]{3,1,2,0:T(8,128)(2,1)}) fusion(bf16[128,2,8,128]{0,3,2,1:T(8,128)(2,1)} %bitcast.122, bf16[2048,2,128,1]{0,2,3,1:T(8,128)(2,1)S(1)} %bitcast.119, f32[2,2048,128,8]{2,1,3,0:T(8,128)} %copy-done, f32[2,8,128]{2,1,0:T(8,128)S(1)} %log_add_fusion, ...), kind=kOutput, calls=%fused_computation.26 | convolution fusion | flops 1096022016 | bytes 19152896 | tf_op jit(solution)/shard_map/giqk,kgd->qgid/dot_general | solution.py:65
  202.6 9.3 %fusion.1 = bf16[2,8,128,2048]{2,3,1,0:T(8,128)(2,1)S(1)} fusion(f32[2,2048,128,8]{2,1,3,0:T(8,128)} %copy-done, f32[2,8,128]{2,1,0:T(8,128)S(1)} %bitcast.128, f32[2,8,128]{2,1,0:T(8,128)S(1)} %log_add_fusion, pred[128,2048]{0,1:T(8,128)(4,1)S(1)} %compare_and_fusion, bf16[2048,2,128,1]{0,2,3,1:T(8,128)(2,1)S(1)} %bitcast.120, ...), kind=kOutput, calls=%fused_computation.2 | convolution fusion | flops 1103101952 | bytes 27017216 | tf_op jit(solution)/shard_map/qgid,kgd->giqk/dot_general | solution.py:71
  211.9 3.2 copy-done.1
  215.1 2.8 fusion.5
  217.9 1.3 copy.75
  219.3 1.7 pad_maximum_fusion.1
  221.0 2.6 copy.77
  223.6 173.1 %all-reduce.2.cloned.1.call-done = bf16[16,128,512]{1,2,0:T(8,128)(2,1)} async-done(((bf16[16,128,512]{1,2,0:T(8,128)(2,1)}), bf16[16,128,512]{1,2,0:T(8,128)(2,1)}) %all-reduce.2.cloned.1.call-update) | async-done | bytes 2097168 | tf_op jit(solution)/shard_map/psum | solution.py:89
  396.7 4.4 %fusion.11 = f32[4,128,512]{1,2,0:T(8,128)} fusion(bf16[16,128,4,128]{3,1,2,0:T(8,128)(2,1)} %all-to-all-done.1, bf16[16,128,512]{1,2,0:T(8,128)(2,1)} %all-reduce.2.cloned.1.call-done), kind=kOutput, calls=%fused_computation.20 | convolution fusion | flops 1073741824 | bytes 5242880 | tf_op jit(solution)/shard_map/ctjb,ctn->jbn/dot_general | solution.py:91
  401.2 4.7 %fusion.14 = bf16[2,128,8,128]{3,1,2,0:T(8,128)(2,1)S(1)} fusion(bf16[2048,2,128,1]{0,2,3,1:T(8,128)(2,1)S(1)} %bitcast.111, bf16[2,8,128,2048]{2,3,1,0:T(8,128)(2,1)} %copy-done.1), kind=kOutput, calls=%fused_computation.22 | convolution fusion | flops 1074266112 | bytes 9961472 | tf_op jit(solution)/shard_map/giqk,kgd->qgid/dot_general | solution.py:76
  405.9 1.0 copy.82
  406.9 1.0 copy.81
  408.0 23.4 %reduce-scatter.2.cloned.1.call-done = f32[1,128,512]{1,2,0:T(8,128)} async-done(((f32[4,128,512]{1,2,0:T(8,128)}), f32[1,128,512]{1,2,0:T(8,128)}) %reduce-scatter.2.cloned.1.call-update) | async-done | bytes 262160 | tf_op jit(solution)/shard_map/reduce_scatter | solution.py:92
  431.4 1.0 fusion.40
  432.4 0.8 copy.83
  (31 shorter events, 1.6 us)
Async XLA Ops:
  7.2 91.5 %all-gather.2.cloned.1.call-start = ((), (), s32[]{:S(2)}) async-start(), calls=%async_computation.3 | async-start | bytes 10485760 | tf_op jit(solution)/shard_map/all_gather | solution.py:40
  105.0 14.2 %copy-start.3 = (bf16[1,128,2048]{2,1,0:T(8,128)(2,1)S(1)}, bf16[1,128,2048]{2,1,0:T(8,128)(2,1)}, u32[]{:S(2)}) copy-start(bf16[1,128,2048]{2,1,0:T(8,128)(2,1)} %param.7) | copy-start | bytes 1572868
  105.0 15.2 %copy-start.4 = (bf16[1,128,2048]{2,1,0:T(8,128)(2,1)S(1)}, bf16[1,128,2048]{2,1,0:T(8,128)(2,1)}, u32[]{:S(2)}) copy-start(bf16[1,128,2048]{2,1,0:T(8,128)(2,1)} %param.8) | copy-start | bytes 1572868
  105.0 20.2 %copy-start.7 = (s32[1,4]{1,0:T(1,128)S(1)}, s32[1,4]{1,0:T(1,128)}, u32[]{:S(2)}) copy-start(s32[1,4]{1,0:T(1,128)} %param.11) | copy-start | bytes 52
  106.8 58.8 %all-to-all-start = ((bf16[16,128,512]{1,2,0:T(8,128)(2,1)}), bf16[16,128,512]{1,2,0:T(8,128)(2,1)S(1)}, u32[]{:S(2)}, u32[]{:S(2)}) async-start(bf16[16,128,512]{1,2,0:T(8,128)(2,1)} %stack.2), calls=%async_computation | async-start | bytes 4194304 | tf_op jit(solution)/shard_map/all_to_all | solution.py:43
  165.6 58.0 %all-to-all-start.1 = ((bf16[16,128,4,128]{3,1,2,0:T(8,128)(2,1)}), bf16[16,128,4,128]{3,1,2,0:T(8,128)(2,1)}, u32[]{:S(2)}, u32[]{:S(2)}) async-start(bf16[16,128,4,128]{3,1,2,0:T(8,128)(2,1)} %copy.79), calls=%async_computation.1 | async-start | bytes 4194304 | tf_op jit(solution)/shard_map/all_to_all | solution.py:38
  170.5 226.3 %all-reduce.2.cloned.1.call-start = ((), (), s32[]{:S(2)}) async-start(), calls=%async_computation.4 | async-start | bytes 4194304 | tf_op jit(solution)/shard_map/psum | solution.py:89
  174.6 5.7 %copy-start = (f32[2,2048,128,8]{2,1,3,0:T(8,128)}, f32[2,2048,128,8]{2,1,3,0:T(8,128)S(1)}, u32[]{:S(2)}) copy-start(f32[2,2048,128,8]{2,1,3,0:T(8,128)S(1)} %get-tuple-element.25) | copy-start | bytes 50331652
  191.8 10.8 %copy-start.5 = (bf16[1,128,2048]{1,2,0:T(8,128)(2,1)S(1)}, bf16[1,128,2048]{1,2,0:T(8,128)(2,1)}, u32[]{:S(2)}) copy-start(bf16[1,128,2048]{1,2,0:T(8,128)(2,1)} %copy.68) | copy-start | bytes 1572868
  202.6 12.5 %copy-start.2 = (bf16[1,128,2048]{1,2,0:T(8,128)(2,1)S(1)}, bf16[1,128,2048]{1,2,0:T(8,128)(2,1)}, u32[]{:S(2)}) copy-start(bf16[1,128,2048]{1,2,0:T(8,128)(2,1)} %copy.101) | copy-start | bytes 1572868
  211.9 3.2 copy-start.1
  223.6 207.8 %reduce-scatter.2.cloned.1.call-start = ((), (), s32[]{:S(2)}) async-start(), calls=%async_computation.5 | async-start | bytes 1310720 | tf_op jit(solution)/shard_map/reduce_scatter | solution.py:92
  401.2 5.7 %copy-start.6 = (bf16[2,128,8,128]{3,1,2,0:T(8,128)(2,1)S(1)}, bf16[2,128,8,128]{3,1,2,0:T(8,128)(2,1)}, u32[]{:S(2)}) copy-start(bf16[2,128,8,128]{3,1,2,0:T(8,128)(2,1)} %get-tuple-element.27) | copy-start | bytes 1572868
Sparse Core Ops, SparseCore 0:
  10.4 88.2 all-gather.1
  223.7 172.9 all-reduce.1
  401.3 30.0 reduce-scatter.1
